TPU v7x, 256 devices: a whole 4x4x8 slice. The times are simulated.
256 devices in a mesh: nodes: 64 (over x, z, core), heads: 4 (over y).
Axes of the slice: x: 4, y: 4, z: 8, core: 2. Of those that a mesh axis runs over, the one named last changes fastest.
Arguments:
- feats: bfloat16 [65536, 512], P('nodes'), may hold values from -6 to 6
- w_query: bfloat16 [512, 512], P(None, 'heads'), may hold values from -0.25 to 0.25
- w_key: bfloat16 [512, 512], P(None, 'heads'), may hold values from -0.25 to 0.25
- w_value: bfloat16 [512, 512], P(None, 'heads'), may hold values from -0.25 to 0.25
- w_out: bfloat16 [512, 512], P('heads'), may hold values from -6 to 6
- head_scale: float32 [8], P('heads'), may hold values from 2 to 10
- nbr_owner: int32 [512, 4], P('nodes'), may hold values from 0 to 63, all different within a row; in each aligned block of 8 rows (0 to 7, 8 to 15, ...) at most 2 rows name the same one
- nbr_local: int32 [512, 4], P('nodes'), may hold values from 0 to 7
- slot_valid: int32 [512, 4], P('nodes'), may hold values 0 or 1
Outputs:
- mixed: bfloat16 [65536, 512], P('nodes', 'heads')
Inputs may be any that keep to these rules, and one draw needn't show every extreme that they name: `nbr_owner`: the 4 owners listed for one query block are distinct. Among the query blocks of one index of nodes, no owner is listed more than 2 times, and 2 is reached.
All inputs are finite; a program needn't handle non-finite values. No bound on the sum of `slot_valid` on one device may be relied on, other than what follows from the above.
Results may differ from a plain program's by a relative error of at most 0.012.
Values may be sent and summed in bfloat16 or wider, within the bound.
No kernel may reach another device: no remote copies, remote signals or barrier semaphores. Data moves between devices by JAX's collectives and lax.ppermute only.
A program may use at most 128 MiB of HBM per device.

v0:
```python
import functools

import jax
import jax.numpy as jnp
from jax import lax
from jax.experimental import pallas as pl
from jax.experimental.pallas import tpu as pltpu
from jax.sharding import PartitionSpec as P


def unit_rows(values, count):
    shaped = values.reshape(values.shape[0], count, -1)
    total = jnp.sum(shaped * shaped, axis=-1, keepdims=True)
    return (shaped * lax.rsqrt(total + 1e-06)).astype(jnp.bfloat16).reshape(values.shape)


def tile_kernel(pick_ref, live_ref, scale_ref, q_ref, kv_ref, num_ref, den_ref, *, count, group):
    g = pl.program_id(0)
    width, feat = q_ref.shape[1], q_ref.shape[2]
    hd = feat // count
    ones = jnp.ones((8, width), jnp.bfloat16)
    nt = (((1,), (1,)), ((), ()))
    for i in range(group):
        t = g * group + i

        @pl.when(live_ref[t] > 0)
        def _():
            q = q_ref[i]
            kv = kv_ref[pick_ref[t]]
            for h in range(count):
                qh = q[:, h * hd:(h + 1) * hd]
                kh = kv[:, h * hd:(h + 1) * hd]
                vh = kv[:, feat + h * hd:feat + (h + 1) * hd]
                s = lax.dot_general(qh, kh, nt, preferred_element_type=jnp.float32)
                w = jnp.exp(scale_ref[h] * (s - 1.0))
                w_hi = w.astype(jnp.bfloat16)
                w_lo = (w - w_hi.astype(jnp.float32)).astype(jnp.bfloat16)
                den = lax.dot_general(ones, w_hi, nt, preferred_element_type=jnp.float32)
                den = den + lax.dot_general(ones, w_lo, nt, preferred_element_type=jnp.float32)
                den_ref[i:i + 1, h * width:(h + 1) * width] = den[0:1]
                num = jnp.dot(w_hi, vh, preferred_element_type=jnp.float32)
                num_ref[i, :, h * hd:(h + 1) * hd] = num.astype(jnp.bfloat16)

        @pl.when(live_ref[t] == 0)
        def _():
            num_ref[i] = jnp.zeros((width, feat), num_ref.dtype)
            den_ref[i:i + 1, :] = jnp.zeros((1, count * width), den_ref.dtype)


def run_tiles(query_tiles, block_pairs, pick, live, scales):
    tiles, width, feat = query_tiles.shape
    count = scales.shape[0]
    group = 8
    nblocks = block_pairs.shape[0]
    grid_spec = pltpu.PrefetchScalarGridSpec(
        num_scalar_prefetch=2,
        grid=(tiles // group,),
        in_specs=[
            pl.BlockSpec(memory_space=pltpu.SMEM),
            pl.BlockSpec((group, width, feat), lambda g, pick, live: (g, 0, 0)),
            pl.BlockSpec((nblocks, width, 2 * feat), lambda g, pick, live: (0, 0, 0)),
        ],
        out_specs=[
            pl.BlockSpec((group, width, feat), lambda g, pick, live: (g, 0, 0)),
            pl.BlockSpec((group, count * width), lambda g, pick, live: (g, 0)),
        ],
    )
    numer, denom = pl.pallas_call(
        functools.partial(tile_kernel, count=count, group=group),
        grid_spec=grid_spec,
        out_shape=[
            jax.ShapeDtypeStruct((tiles, width, feat), jnp.bfloat16),
            jax.ShapeDtypeStruct((tiles, count * width), jnp.float32),
        ],
    )(pick, live, scales, query_tiles, block_pairs)
    return numer, denom.astype(jnp.bfloat16)


def body(feats, w_query, w_key, w_value, w_out, head_scale, nbr_owner, nbr_local, slot_valid):
    rows = feats.shape[0]
    feat = w_query.shape[1]
    count = head_scale.shape[0]
    nblocks, slots = nbr_owner.shape
    width = rows // nblocks
    devices = lax.axis_size("nodes")
    capacity = max(2, min(nblocks // 2, 3 * nblocks * slots // (2 * devices)))
    tile_count = devices * capacity
    query_n = unit_rows(jnp.dot(feats, w_query, preferred_element_type=jnp.float32), count)
    key_n = unit_rows(jnp.dot(feats, w_key, preferred_element_type=jnp.float32), count)
    value_b = jnp.dot(feats, w_value, preferred_element_type=jnp.float32).astype(jnp.bfloat16)
    query_block_rows = query_n.reshape(nblocks, width, feat)
    block_pair_list = jnp.concatenate([key_n, value_b], axis=1).reshape(nblocks, width, 2 * feat)
    owners = nbr_owner.reshape(-1)
    pairs = owners.shape[0]
    pair_block = jnp.arange(pairs, dtype=jnp.int32) // slots
    owner_hot = (owners[:, None] == jnp.arange(devices, dtype=jnp.int32)[None, :]).astype(jnp.int32)
    rank = jnp.sum(jnp.cumsum(owner_hot, axis=0) * owner_hot, axis=1) - 1
    target = owners * capacity + rank
    place = (target[:, None] == jnp.arange(tile_count, dtype=jnp.int32)[None, :]).astype(jnp.int32)
    wanted = jnp.where(slot_valid.reshape(-1) > 0, nbr_local.reshape(-1), -1)
    request = jnp.sum(place * (wanted[:, None] + 1), axis=0) - 1
    block_hot = (pair_block[:, None] == jnp.arange(nblocks, dtype=jnp.int32)[None, :]).astype(
        jnp.float32
    )
    selector_onehot = jnp.dot(place.T.astype(jnp.float32), block_hot).astype(jnp.bfloat16)
    query_outgoing = jnp.einsum(
        "cm,mqk->cqk", selector_onehot, query_block_rows, preferred_element_type=jnp.float32
    ).astype(jnp.bfloat16)
    asked = lax.all_to_all(
        request.reshape(devices, capacity), "nodes", split_axis=0, concat_axis=0, tiled=True
    ).reshape(-1)
    query_in = lax.all_to_all(
        query_outgoing.reshape(devices, capacity * width, feat),
        "nodes",
        split_axis=0,
        concat_axis=0,
        tiled=True,
    )
    self_numer, self_denom = run_tiles(
        query_block_rows,
        block_pair_list,
        jnp.arange(nblocks, dtype=jnp.int32),
        jnp.ones((nblocks,), jnp.int32),
        head_scale,
    )
    live_in = (asked >= 0).astype(jnp.int32)
    pick_in = jnp.clip(asked, 0, nblocks - 1)
    numer, denom = run_tiles(
        query_in.reshape(tile_count, width, feat), block_pair_list, pick_in, live_in, head_scale
    )
    numer = lax.all_to_all(
        numer.reshape(devices, capacity * width, feat),
        "nodes",
        split_axis=0,
        concat_axis=0,
        tiled=True,
    )
    denom = lax.all_to_all(
        denom.reshape(devices, capacity * count * width),
        "nodes",
        split_axis=0,
        concat_axis=0,
        tiled=True,
    )
    numer_total = self_numer.astype(jnp.float32) + jnp.einsum(
        "uq,upl->qpl",
        selector_onehot,
        numer.reshape(tile_count, width, feat),
        preferred_element_type=jnp.float32,
    )
    denominator_overall = self_denom.astype(jnp.float32) + jnp.einsum(
        "uq,ul->ql",
        selector_onehot,
        denom.reshape(tile_count, count * width),
        preferred_element_type=jnp.float32,
    )
    den_rows = jnp.transpose(denominator_overall.reshape(nblocks, count, width), (0, 2, 1))
    attn = numer_total.reshape(nblocks, width, count, feat // count) / den_rows[..., None]
    attn = attn.astype(jnp.bfloat16).reshape(rows, feat)
    attn_all = lax.all_gather(attn, "heads", axis=1, tiled=True)
    cols = w_out.shape[0]
    w_out_t = lax.all_gather(w_out.T, "heads", axis=1, tiled=True)
    w_cols = lax.dynamic_slice_in_dim(w_out_t, lax.axis_index("heads") * cols, cols, axis=0).T
    return jnp.dot(attn_all, w_cols, preferred_element_type=jnp.float32).astype(jnp.bfloat16)


def solution(mesh):
    placed = (
        P("nodes", None),
        P(None, "heads"),
        P(None, "heads"),
        P(None, "heads"),
        P("heads", None),
        P("heads"),
        P("nodes", None),
        P("nodes", None),
        P("nodes", None),
    )
    return jax.shard_map(
        body, mesh=mesh, in_specs=placed, out_specs=P("nodes", "heads"), check_vma=False
    )
```

profile of v0, /device:TPU:2, one launch (start us, length us, event | category | flops | bytes accessed | tf_op | source)
XLA Modules:
  0.0 349.6 jit_solution(7369735990612615916)
XLA Ops:
  6.5 0.0 copy-start
  6.5 0.8 copy.56
  7.4 0.1 reshape.127
  7.5 0.1 fusion.10
  7.5 0.1 reduce_window_sum.11
  7.6 0.2 select_reduce_fusion.1
  7.8 0.7 select_add_fusion
  8.5 0.1 copy.57
  8.6 0.1 add.68
  8.7 0.1 select_reduce_fusion
  8.8 0.7 sub.19
  9.5 12.0 %all-to-all-start = ((s32[64,1,2]{2,1,0:T(1,128)}), s32[64,1,2]{2,1,0:T(1,128)S(1)}, u32[]{:S(2)}, u32[]{:S(2)}) async-start(s32[64,1,2]{2,1,0:T(1,128)} %bitcast.7), calls=%async_computation | async-start | bytes 65536 | tf_op jit(solution)/shard_map/all_to_all | solution.py:109
  21.5 0.2 convolution_convert_fusion.3
  21.8 0.0 copy-done
  21.8 1.4 fusion.15
  23.1 0.2 copy.52
  23.5 0.1 copy.65
  23.6 0.2 copy.53
  23.8 0.1 multiply_convert_fusion.1.q_ref
  23.9 0.0 copy-start.1
  23.9 1.3 convolution_convert_fusion
  25.2 4.6 %copy.60 = bf16[128,128,128]{2,1,0:T(8,128)(2,1)} copy(bf16[128,128,128]{2,0,1:T(8,128)(2,1)S(1)} %convolution_convert_fusion) | data formatting | bytes 8388608 | tf_op jit(solution)/shard_map/convert_element_type | solution.py:108
  29.8 0.0 copy-done.1
  29.8 0.3 all-to-all-done
  30.1 0.0 copy-start.3
  30.1 10.3 %all-to-all-start.1 = ((bf16[64,256,128]{2,1,0:T(8,128)(2,1)}), bf16[64,256,128]{2,1,0:T(8,128)(2,1)}, u32[]{:S(2)}, u32[]{:S(2)}) async-start(bf16[64,256,128]{2,1,0:T(8,128)(2,1)} %bitcast.46), calls=%async_computation.1 | async-start | bytes 8388608 | tf_op jit(solution)/shard_map/all_to_all | solution.py:112
  40.5 0.0 copy-done.3
  40.5 0.0 copy-start.5
  40.5 0.4 fusion.16
  40.9 0.2 copy.54
  41.2 0.2 copy.55
  41.4 0.1 multiply_convert_fusion
  41.5 0.0 copy-done.5
  41.5 0.4 convolution_convert_fusion.2
  41.9 0.9 pad_maximum_fusion.kv_ref
  42.9 0.2 fusion.8
  43.1 0.7 min.12.pick_ref
  43.8 0.6 reshape.135.live_ref
  44.4 90.9 %all-to-all-done.1 = bf16[64,256,128]{2,1,0:T(8,128)(2,1)} async-done(((bf16[64,256,128]{2,1,0:T(8,128)(2,1)}), bf16[64,256,128]{2,1,0:T(8,128)(2,1)}, u32[]{:S(2)}, u32[]{:S(2)}) %all-to-all-start.1) | async-done | bytes 4194336 | tf_op jit(solution)/shard_map/all_to_all | solution.py:112
  135.3 19.9 %shard_map.92 = (bf16[128,128,128]{2,1,0:T(8,128)(2,1)}, f32[128,256]{1,0:T(8,128)}) custom-call(s32[128]{0:T(128)} %min.12.pick_ref, s32[128]{0:T(128)} %reshape.135.live_ref, f32[2]{0:T(128)} %scale_ref.3, bf16[128,128,128]{2,1,0:T(8,128)(2,1)} %bitcast.9.q_ref, bf16[8,128,256]{2,1,0:T(8,128)(2,1)} %pad_maximum_fusion.kv_ref), custom_call_target="tpu_custom_call" | custom-call | tf_op jit(solution)/shard_map/pallas_call | solution.py:68
  155.3 0.9 convert_element_type.65
  156.2 0.5 broadcast.126
  156.7 1.0 reduce.9
  157.7 50.8 %all_to_all.26 = bf16[64,2,256]{2,1,0:T(2,128)(2,1)S(1)} all-to-all(bf16[64,2,256]{2,1,0:T(2,128)(2,1)S(1)} %reshape.150), channel_id=1, replica_groups=mesh['nodes'=64,'heads'=4] {'nodes'}, dimensions={0} | all-to-all | bytes 131072 | tf_op jit(solution)/shard_map/all_to_all | solution.py:138
  208.6 6.5 %all-to-all-start.2 = ((bf16[64,256,128]{2,1,0:T(8,128)(2,1)}), bf16[64,256,128]{2,1,0:T(8,128)(2,1)}, u32[]{:S(2)}, u32[]{:S(2)}) async-start(bf16[64,256,128]{2,1,0:T(8,128)(2,1)} %bitcast.47), calls=%async_computation.2 | async-start | bytes 8388608 | tf_op jit(solution)/shard_map/all_to_all | solution.py:131
  215.1 0.0 all-gather.2.cloned.1.call-start
  215.1 0.5 iota.21.pick_ref
  215.6 0.6 broadcast_2_live_ref.2.live_ref
  216.2 6.8 %shard_map.91 = (bf16[8,128,128]{2,1,0:T(8,128)(2,1)}, f32[8,256]{1,0:T(8,128)}) custom-call(s32[8]{0:T(128)} %iota.21.pick_ref, s32[8]{0:T(128)} %broadcast_2_live_ref.2.live_ref, f32[2]{0:T(128)} %scale_ref.3, bf16[8,128,128]{2,1,0:T(8,128)(2,1)} %copy-done.1, bf16[8,128,256]{2,1,0:T(8,128)(2,1)} %pad_maximum_fusion.kv_ref), custom_call_target="tpu_custom_call" | custom-call | tf_op jit(solution)/shard_map/pallas_call | solution.py:68
  223.1 0.0 copy-start.2
  223.1 0.1 reshape.151
  223.1 0.4 reduce.2
  223.5 0.8 fusion.2
  224.4 85.6 %all-to-all-done.2 = bf16[64,256,128]{2,1,0:T(8,128)(2,1)} async-done(((bf16[64,256,128]{2,1,0:T(8,128)(2,1)}), bf16[64,256,128]{2,1,0:T(8,128)(2,1)}, u32[]{:S(2)}, u32[]{:S(2)}) %all-to-all-start.2) | async-done | bytes 4194336 | tf_op jit(solution)/shard_map/all_to_all | solution.py:131
  309.9 4.5 %fusion = f32[8,128,128]{2,0,1:T(8,128)S(1)} fusion(bf16[128,128,128]{2,1,0:T(8,128)(2,1)} %bitcast.11, bf16[128,8]{0,1:T(8,128)(2,1)S(1)} %convolution_convert_fusion.3), kind=kOutput, calls=%fused_computation | convolution fusion | flops 33554432 | bytes 4720640 | tf_op jit(solution)/shard_map/uq,upl->qpl/dot_general | solution.py:145
  314.5 0.0 copy-done.2
  314.5 0.1 copy_add_fusion
  314.6 0.2 copy.64
  314.8 0.8 fusion.3
  315.6 0.0 all-gather.2.cloned.1.call-update
  315.7 0.0 copy-done.4
  315.7 14.1 %all_gather.7 = bf16[512,512]{0,1:T(8,128)(2,1)S(1)} all-gather(bf16[512,128]{0,1:T(8,128)(2,1)S(1)} %bitcast.56), channel_id=1, replica_groups=mesh['nodes'=64,'heads'=4] {'heads'}, dimensions={1}, use_global_device_ids=true | all-gather | bytes 655360 | tf_op jit(solution)/shard_map/all_gather | solution.py:162
  329.8 10.5 %all-gather.2.cloned.1.call-done = bf16[1024,512]{0,1:T(8,128)(2,1)} async-done(((bf16[1024,128]{0,1:T(8,128)(2,1)}), bf16[1024,512]{0,1:T(8,128)(2,1)}) %all-gather.2.cloned.1.call-update) | async-done | bytes 1048592 | tf_op jit(solution)/shard_map/all_gather | solution.py:160
  340.3 2.4 convolution_convert_fusion.1
  (13 shorter events, 0.3 us)
Async XLA Ops:
  6.5 15.2 %copy-start = (bf16[1024,512]{1,0:T(8,128)(2,1)S(1)}, bf16[1024,512]{1,0:T(8,128)(2,1)}, u32[]{:S(2)}) copy-start(bf16[1024,512]{1,0:T(8,128)(2,1)} %param.9) | copy-start | bytes 3145732
  9.5 20.6 %all-to-all-start = ((s32[64,1,2]{2,1,0:T(1,128)}), s32[64,1,2]{2,1,0:T(1,128)S(1)}, u32[]{:S(2)}, u32[]{:S(2)}) async-start(s32[64,1,2]{2,1,0:T(1,128)} %bitcast.7), calls=%async_computation | async-start | bytes 65536 | tf_op jit(solution)/shard_map/all_to_all | solution.py:109
  23.9 5.9 %copy-start.1 = (bf16[8,128,128]{2,1,0:T(8,128)(2,1)}, bf16[8,128,128]{2,1,0:T(8,128)(2,1)S(1)}, u32[]{:S(2)}) copy-start(bf16[8,128,128]{2,1,0:T(8,128)(2,1)S(1)} %multiply_convert_fusion.1.q_ref) | copy-start | bytes 786436
  30.1 10.3 %copy-start.3 = (bf16[512,128]{1,0:T(8,128)(2,1)S(1)}, bf16[512,128]{1,0:T(8,128)(2,1)}, u32[]{:S(2)}) copy-start(bf16[512,128]{1,0:T(8,128)(2,1)} %param.11) | copy-start | bytes 393220
  30.1 105.2 %all-to-all-start.1 = ((bf16[64,256,128]{2,1,0:T(8,128)(2,1)}), bf16[64,256,128]{2,1,0:T(8,128)(2,1)}, u32[]{:S(2)}, u32[]{:S(2)}) async-start(bf16[64,256,128]{2,1,0:T(8,128)(2,1)} %bitcast.46), calls=%async_computation.1 | async-start | bytes 8388608 | tf_op jit(solution)/shard_map/all_to_all | solution.py:112
  40.5 1.0 copy-start.5
  208.6 101.4 %all-to-all-start.2 = ((bf16[64,256,128]{2,1,0:T(8,128)(2,1)}), bf16[64,256,128]{2,1,0:T(8,128)(2,1)}, u32[]{:S(2)}, u32[]{:S(2)}) async-start(bf16[64,256,128]{2,1,0:T(8,128)(2,1)} %bitcast.47), calls=%async_computation.2 | async-start | bytes 8388608 | tf_op jit(solution)/shard_map/all_to_all | solution.py:131
  215.1 125.2 %all-gather.2.cloned.1.call-start = ((), (), s32[]{:S(2)}) async-start(), calls=%async_computation.4 | async-start | bytes 1310720 | tf_op jit(solution)/shard_map/all_gather | solution.py:160
  223.1 91.4 %copy-start.2 = (bf16[8,128,128]{2,1,0:T(8,128)(2,1)S(1)}, bf16[8,128,128]{2,1,0:T(8,128)(2,1)}, u32[]{:S(2)}) copy-start(bf16[8,128,128]{2,1,0:T(8,128)(2,1)} %get-tuple-element.9) | copy-start | bytes 786436
  309.9 5.7 %copy-start.4 = (bf16[128,512]{1,0:T(8,128)(2,1)S(1)}, bf16[128,512]{1,0:T(8,128)(2,1)}, u32[]{:S(2)}) copy-start(bf16[128,512]{1,0:T(8,128)(2,1)} %param.13) | copy-start | bytes 393220
Sparse Core Ops, SparseCore 0:
  315.8 24.4 all-gather.1
where the time goes:
time: 351 us; the launch traced here: 350 us
  waiting for transfers between devices  187 us (53%)
  blocking collectives  64.9 us (18%)
  starting transfers between devices  28.9 us (8%)
  Pallas kernels  26.8 us (8%)
  between operations  13.7 us (4%)
  matrix products  11.5 us (3%)
  local copies, waits for them, and re-layouts  10.9 us (3%)
  other arithmetic  5.67 us (2%)
    all_to_all x1, waiting for transfers between devices, body(): lax.all_to_all(query_outgoing.reshape(devices, capacity * width, feat), '...  90.9 us
    all_to_all x1, waiting for transfers between devices, body(): lax.all_to_all(numer.reshape(devices, capacity * width, feat), 'nodes', s...  85.6 us
    all_to_all x1, blocking collectives, body(): lax.all_to_all(denom.reshape(devices, capacity * count * width), 'nodes',...  50.8 us
    pallas_call x2, Pallas kernels, run_tiles(): pl.pallas_call(functools.partial(tile_kernel, count=count, group=group),...  26.8 us
    all_gather x1, blocking collectives, body(): w_out_t = lax.all_gather(w_out.T, 'heads', axis=1, tiled=True)  14.1 us
    all_to_all x1, starting transfers between devices, body(): lax.all_to_all(request.reshape(devices, capacity), 'nodes', split_axis=0,...  12 us
    all_gather x1, waiting for transfers between devices, body(): attn_all = lax.all_gather(attn, 'heads', axis=1, tiled=True)  10.5 us
    all_to_all x1, starting transfers between devices, body(): lax.all_to_all(query_outgoing.reshape(devices, capacity * width, feat), '...  10.3 us
  transfers between devices with their start and end apart: 4, of which 4 were waited for; matrix products, arithmetic and copies ran while one was open for 4% of the time, Pallas kernels for 2%

commit v1 on v0

--- a/solution.py
+++ b/solution.py
@@ -14,14 +14,16 @@
     return (shaped * lax.rsqrt(total + 1e-06)).astype(jnp.bfloat16).reshape(values.shape)
 
 
-def tile_kernel(pick_ref, live_ref, scale_ref, q_ref, kv_ref, num_ref, den_ref, *, count, group):
+def tile_kernel(pick_ref, live_ref, scale_ref, q_ref, kv_ref, out_ref, den_scr, *, count, capacity):
     g = pl.program_id(0)
     width, feat = q_ref.shape[1], q_ref.shape[2]
+    group = q_ref.shape[0]
     hd = feat // count
     ones = jnp.ones((8, width), jnp.bfloat16)
     nt = (((1,), (1,)), ((), ()))
     for i in range(group):
         t = g * group + i
+        dest, slot = i // capacity, i % capacity
 
         @pl.when(live_ref[t] > 0)
         def _():
@@ -37,21 +39,32 @@
                 w_lo = (w - w_hi.astype(jnp.float32)).astype(jnp.bfloat16)
                 den = lax.dot_general(ones, w_hi, nt, preferred_element_type=jnp.float32)
                 den = den + lax.dot_general(ones, w_lo, nt, preferred_element_type=jnp.float32)
-                den_ref[i:i + 1, h * width:(h + 1) * width] = den[0:1]
+                den_scr[i * count + h:i * count + h + 1, :] = den[0:1]
                 num = jnp.dot(w_hi, vh, preferred_element_type=jnp.float32)
-                num_ref[i, :, h * hd:(h + 1) * hd] = num.astype(jnp.bfloat16)
+                out_ref[dest, slot * width:(slot + 1) * width, h * hd:(h + 1) * hd] = num.astype(
+                    jnp.bfloat16
+                )
 
         @pl.when(live_ref[t] == 0)
         def _():
-            num_ref[i] = jnp.zeros((width, feat), num_ref.dtype)
-            den_ref[i:i + 1, :] = jnp.zeros((1, count * width), den_ref.dtype)
+            out_ref[dest, slot * width:(slot + 1) * width, :] = jnp.zeros((width, feat), out_ref.dtype)
+            den_scr[i * count:(i + 1) * count, :] = jnp.zeros((count, width), den_scr.dtype)
+
+    per = capacity * count
+    extra = out_ref.shape[1] - capacity * width
+    for d in range(group // capacity):
+        rows = den_scr[d * per:(d + 1) * per, :]
+        block = jnp.concatenate([rows, jnp.zeros((extra - per, width), rows.dtype)], axis=0)
+        out_ref[d, capacity * width:, :] = block.astype(out_ref.dtype)
 
 
-def run_tiles(query_tiles, block_pairs, pick, live, scales):
+def run_tiles(query_tiles, block_pairs, pick, live, scales, capacity):
     tiles, width, feat = query_tiles.shape
     count = scales.shape[0]
     group = 8
     nblocks = block_pairs.shape[0]
+    extra = 16
+    rows_out = capacity * width + extra
     grid_spec = pltpu.PrefetchScalarGridSpec(
         num_scalar_prefetch=2,
         grid=(tiles // group,),
@@ -60,20 +73,21 @@
             pl.BlockSpec((group, width, feat), lambda g, pick, live: (g, 0, 0)),
             pl.BlockSpec((nblocks, width, 2 * feat), lambda g, pick, live: (0, 0, 0)),
         ],
-        out_specs=[
-            pl.BlockSpec((group, width, feat), lambda g, pick, live: (g, 0, 0)),
-            pl.BlockSpec((group, count * width), lambda g, pick, live: (g, 0)),
-        ],
+        out_specs=pl.BlockSpec((group // capacity, rows_out, feat), lambda g, pick, live: (g, 0, 0)),
+        scratch_shapes=[pltpu.VMEM((group * count, width), jnp.float32)],
     )
-    numer, denom = pl.pallas_call(
-        functools.partial(tile_kernel, count=count, group=group),
+    return pl.pallas_call(
+        functools.partial(tile_kernel, count=count, capacity=capacity),
         grid_spec=grid_spec,
-        out_shape=[
-            jax.ShapeDtypeStruct((tiles, width, feat), jnp.bfloat16),
-            jax.ShapeDtypeStruct((tiles, count * width), jnp.float32),
-        ],
+        out_shape=jax.ShapeDtypeStruct((tiles // capacity, rows_out, feat), jnp.bfloat16),
     )(pick, live, scales, query_tiles, block_pairs)
-    return numer, denom.astype(jnp.bfloat16)
+
+
+def split_result(result, capacity, width, count):
+    dests, _, feat = result.shape
+    numer = result[:, :capacity * width, :].reshape(dests * capacity, width, feat)
+    denom = result[:, capacity * width:capacity * width + capacity * count, :]
+    return numer, denom.reshape(dests * capacity, count * width)
 
 
 def body(feats, w_query, w_key, w_value, w_out, head_scale, nbr_owner, nbr_local, slot_valid):
@@ -116,52 +130,49 @@
         concat_axis=0,
         tiled=True,
     )
-    self_numer, self_denom = run_tiles(
-        query_block_rows,
-        block_pair_list,
-        jnp.arange(nblocks, dtype=jnp.int32),
-        jnp.ones((nblocks,), jnp.int32),
-        head_scale,
+    self_numer, self_denom = split_result(
+        run_tiles(
+            query_block_rows,
+            block_pair_list,
+            jnp.arange(nblocks, dtype=jnp.int32),
+            jnp.ones((nblocks,), jnp.int32),
+            head_scale,
+            capacity,
+        ),
+        capacity,
+        width,
+        count,
     )
     live_in = (asked >= 0).astype(jnp.int32)
     pick_in = jnp.clip(asked, 0, nblocks - 1)
-    numer, denom = run_tiles(
-        query_in.reshape(tile_count, width, feat), block_pair_list, pick_in, live_in, head_scale
+    result = run_tiles(
+        query_in.reshape(tile_count, width, feat),
+        block_pair_list,
+        pick_in,
+        live_in,
+        head_scale,
+        capacity,
     )
-    numer = lax.all_to_all(
-        numer.reshape(devices, capacity * width, feat),
-        "nodes",
-        split_axis=0,
-        concat_axis=0,
-        tiled=True,
-    )
-    denom = lax.all_to_all(
-        denom.reshape(devices, capacity * count * width),
-        "nodes",
-        split_axis=0,
-        concat_axis=0,
-        tiled=True,
-    )
+    result = lax.all_to_all(result, "nodes", split_axis=0, concat_axis=0, tiled=True)
+    numer, denom = split_result(result, capacity, width, count)
     numer_total = self_numer.astype(jnp.float32) + jnp.einsum(
-        "uq,upl->qpl",
-        selector_onehot,
-        numer.reshape(tile_count, width, feat),
-        preferred_element_type=jnp.float32,
+        "uq,upl->qpl", selector_onehot, numer, preferred_element_type=jnp.float32
     )
     denominator_overall = self_denom.astype(jnp.float32) + jnp.einsum(
-        "uq,ul->ql",
-        selector_onehot,
-        denom.reshape(tile_count, count * width),
-        preferred_element_type=jnp.float32,
+        "uq,ul->ql", selector_onehot, denom, preferred_element_type=jnp.float32
     )
     den_rows = jnp.transpose(denominator_overall.reshape(nblocks, count, width), (0, 2, 1))
     attn = numer_total.reshape(nblocks, width, count, feat // count) / den_rows[..., None]
     attn = attn.astype(jnp.bfloat16).reshape(rows, feat)
-    attn_all = lax.all_gather(attn, "heads", axis=1, tiled=True)
     cols = w_out.shape[0]
-    w_out_t = lax.all_gather(w_out.T, "heads", axis=1, tiled=True)
-    w_cols = lax.dynamic_slice_in_dim(w_out_t, lax.axis_index("heads") * cols, cols, axis=0).T
-    return jnp.dot(attn_all, w_cols, preferred_element_type=jnp.float32).astype(jnp.bfloat16)
+    gathered = lax.all_gather(
+        jnp.concatenate([attn, w_out.T], axis=0), "heads", axis=1, tiled=True
+    )
+    attn_all = gathered[:rows]
+    w_rows = lax.dynamic_slice_in_dim(gathered[rows:], lax.axis_index("heads") * cols, cols, axis=0)
+    return lax.dot_general(
+        attn_all, w_rows, (((1,), (1,)), ((), ())), preferred_element_type=jnp.float32
+    ).astype(jnp.bfloat16)
 
 
 def solution(mesh):

time: 351 us -> 347 us (0.989)
  blocking collectives: 64.9 us -> 0 us
  starting transfers between devices: 28.9 us -> 64.3 us
  waiting for transfers between devices: 187 us -> 213 us
  local copies, waits for them, and re-layouts: 10.9 us -> 15.9 us
    all_to_all x1 -> x0, blocking collectives: 50.8 us -> none  [body(): lax.all_to_all(denom.reshape(devices, capacity * count * width), 'nodes',...]
    all_to_all x1, starting transfers between devices: 6.49 us -> 41.9 us  [body(): lax.all_to_all(result, 'nodes', split_axis=0, concat_axis=0, tiled=True)]
    all_gather x1, waiting for transfers between devices: 10.5 us -> 30.7 us  [body(): lax.all_gather(jnp.concatenate([attn, w_out.T], axis=0), 'heads', axis=1,...]
    all_gather x1 -> x0, blocking collectives: 14.1 us -> none  [body(): w_out_t = lax.all_gather(w_out.T, 'heads', axis=1, tiled=True)]
    slice x0 -> x4, local copies, waits for them, and re-layouts: none -> 5.43 us  [the longest x2 3.43 us: split_result(): result[:, :capacity * width, :].reshape(dests * capacity, width, feat)]
    all_to_all x1, waiting for transfers between devices: 85.6 us -> 90.5 us  [body(): lax.all_to_all(result, 'nodes', split_axis=0, concat_axis=0, tiled=True)]
where the time goes in v1:
time: 347 us; the launch traced here: 346 us
  waiting for transfers between devices  213 us (61%)
  starting transfers between devices  64.3 us (19%)
  Pallas kernels  27 us (8%)
  local copies, waits for them, and re-layouts  15.9 us (5%)
  between operations  13.7 us (4%)
  matrix products  8.74 us (3%)
  other arithmetic  4.15 us (1%)
    all_to_all x1, waiting for transfers between devices, body(): lax.all_to_all(query_outgoing.reshape(devices, capacity * width, feat), '...  90.9 us
    all_to_all x1, waiting for transfers between devices, body(): lax.all_to_all(result, 'nodes', split_axis=0, concat_axis=0, tiled=True)  90.5 us
    all_to_all x1, starting transfers between devices, body(): lax.all_to_all(result, 'nodes', split_axis=0, concat_axis=0, tiled=True)  41.9 us
    all_gather x1, waiting for transfers between devices, body(): lax.all_gather(jnp.concatenate([attn, w_out.T], axis=0), 'heads', axis=1,...  30.7 us
    pallas_call x2, Pallas kernels, run_tiles(): pl.pallas_call(functools.partial(tile_kernel, count=count, capacity=capac...  27 us
    all_to_all x1, starting transfers between devices, body(): lax.all_to_all(request.reshape(devices, capacity), 'nodes', split_axis=0,...  12 us
    all_to_all x1, starting transfers between devices, body(): lax.all_to_all(query_outgoing.reshape(devices, capacity * width, feat), '...  10.3 us
  transfers between devices with their start and end apart: 4, of which 4 were waited for; matrix products, arithmetic and copies ran while one was open for 4% of the time, Pallas kernels for 2%

profile of v1, /device:TPU:2, one launch (start us, length us, event | category | flops | bytes accessed | tf_op | source)
XLA Modules:
  0.0 346.2 jit_solution(11653704900492003242)
XLA Ops:
  6.5 0.0 copy-start
  6.5 0.8 copy.48
  7.4 0.1 reshape.125
  7.5 0.1 fusion.14
  7.5 0.1 reduce_window_sum.11
  7.6 0.2 select_reduce_fusion.1
  7.8 0.7 select_add_fusion
  8.5 0.1 copy.49
  8.6 0.1 add.68
  8.7 0.1 select_reduce_fusion
  8.8 0.7 sub.19
  9.5 12.0 %all-to-all-start = ((s32[64,1,2]{2,1,0:T(1,128)}), s32[64,1,2]{2,1,0:T(1,128)S(1)}, u32[]{:S(2)}, u32[]{:S(2)}) async-start(s32[64,1,2]{2,1,0:T(1,128)} %bitcast.8), calls=%async_computation | async-start | bytes 65536 | tf_op jit(solution)/shard_map/all_to_all | solution.py:123
  21.5 0.0 copy-done
  21.5 1.3 fusion.19
  22.9 0.2 copy.44
  23.2 0.1 copy.58
  23.3 0.2 copy.45
  23.6 0.2 convolution_convert_fusion.3
  23.8 0.1 multiply_convert_fusion.1.q_ref
  23.9 0.0 copy-start.1
  23.9 1.3 convolution_convert_fusion
  25.2 4.6 %copy.52 = bf16[128,128,128]{2,1,0:T(8,128)(2,1)} copy(bf16[128,128,128]{2,0,1:T(8,128)(2,1)S(1)} %convolution_convert_fusion) | data formatting | bytes 8388608 | tf_op jit(solution)/shard_map/convert_element_type | solution.py:122
  29.8 0.0 copy-done.1
  29.8 0.3 all-to-all-done
  30.1 0.0 copy-start.2
  30.1 10.3 %all-to-all-start.1 = ((bf16[64,256,128]{2,1,0:T(8,128)(2,1)}), bf16[64,256,128]{2,1,0:T(8,128)(2,1)}, u32[]{:S(2)}, u32[]{:S(2)}) async-start(bf16[64,256,128]{2,1,0:T(8,128)(2,1)} %bitcast.48), calls=%async_computation.1 | async-start | bytes 8388608 | tf_op jit(solution)/shard_map/all_to_all | solution.py:126
  40.5 0.0 copy-done.2
  40.5 0.0 copy-start.4
  40.5 0.4 fusion.20
  40.9 0.2 copy.46
  41.3 0.2 copy.47
  41.4 0.1 multiply_convert_fusion
  41.5 0.0 copy-done.4
  41.5 0.4 convolution_convert_fusion.2
  42.0 0.9 pad_maximum_fusion.kv_ref
  42.9 0.2 fusion.12
  43.1 0.7 min.12.pick_ref
  43.8 0.6 reshape.133.live_ref
  44.4 90.9 %all-to-all-done.1 = bf16[64,256,128]{2,1,0:T(8,128)(2,1)} async-done(((bf16[64,256,128]{2,1,0:T(8,128)(2,1)}), bf16[64,256,128]{2,1,0:T(8,128)(2,1)}, u32[]{:S(2)}, u32[]{:S(2)}) %all-to-all-start.1) | async-done | bytes 4194336 | tf_op jit(solution)/shard_map/all_to_all | solution.py:126
  135.3 20.0 %shard_map.92 = bf16[64,272,128]{2,1,0:T(8,128)(2,1)} custom-call(s32[128]{0:T(128)} %min.12.pick_ref, s32[128]{0:T(128)} %reshape.133.live_ref, f32[2]{0:T(128)} %scale_ref.3, bf16[128,128,128]{2,1,0:T(8,128)(2,1)} %bitcast.10.q_ref, bf16[8,128,256]{2,1,0:T(8,128)(2,1)} %pad_maximum_fusion.kv_ref), custom_call_target="tpu_custom_call" | custom-call | tf_op jit(solution)/shard_map/pallas_call | solution.py:79
  155.3 0.0 copy-start.3
  155.3 41.9 %all-to-all-start.2 = ((bf16[64,272,128]{2,1,0:T(8,128)(2,1)}), bf16[64,272,128]{2,1,0:T(8,128)(2,1)}, u32[]{:S(2)}, u32[]{:S(2)}) async-start(bf16[64,272,128]{2,1,0:T(8,128)(2,1)} %shard_map.92), calls=%async_computation.2 | async-start | bytes 8912896 | tf_op jit(solution)/shard_map/all_to_all | solution.py:156
  197.2 0.0 all-gather.2.cloned.1.call-start
  197.3 0.0 copy-done.3
  197.3 0.1 copy.57
  197.4 0.6 iota.21.pick_ref
  198.0 0.5 broadcast_2_live_ref.2.live_ref
  198.4 7.0 %shard_map.91 = bf16[4,272,128]{2,1,0:T(8,128)(2,1)} custom-call(s32[8]{0:T(128)} %iota.21.pick_ref, s32[8]{0:T(128)} %broadcast_2_live_ref.2.live_ref, f32[2]{0:T(128)} %scale_ref.3, bf16[8,128,128]{2,1,0:T(8,128)(2,1)} %copy-done.1, bf16[8,128,256]{2,1,0:T(8,128)(2,1)} %pad_maximum_fusion.kv_ref), custom_call_target="tpu_custom_call" | custom-call | tf_op jit(solution)/shard_map/pallas_call | solution.py:79
  205.5 1.0 slice.24
  206.4 0.7 slice_convert_fusion
  207.2 90.5 %all-to-all-done.2 = bf16[64,272,128]{2,1,0:T(8,128)(2,1)} async-done(((bf16[64,272,128]{2,1,0:T(8,128)(2,1)}), bf16[64,272,128]{2,1,0:T(8,128)(2,1)}, u32[]{:S(2)}, u32[]{:S(2)}) %all-to-all-start.2) | async-done | bytes 4456480 | tf_op jit(solution)/shard_map/all_to_all | solution.py:156
  297.7 0.9 slice.27
  298.7 0.1 fusion.5
  298.9 0.1 copy.68
  299.0 0.2 copy.56
  299.2 2.5 slice.25
  301.7 2.5 fusion.2
  304.2 0.1 copy.55
  304.3 0.1 fusion.7
  304.4 0.8 pad_maximum_fusion.1
  305.2 0.0 all-gather.2.cloned.1.call-update
  305.2 30.7 %all-gather.2.cloned.1.call-done = bf16[1536,512]{1,0:T(8,128)(2,1)} async-done(((bf16[1536,128]{1,0:T(8,128)(2,1)}), bf16[1536,512]{1,0:T(8,128)(2,1)}) %all-gather.2.cloned.1.call-update) | async-done | bytes 1572880 | tf_op jit(solution)/shard_map/all_gather | solution.py:168
  336.0 1.1 slice.29
  337.0 2.4 convolution_convert_fusion.1
  (12 shorter events, 0.4 us)
Async XLA Ops:
  6.5 15.0 %copy-start = (bf16[1024,512]{1,0:T(8,128)(2,1)S(1)}, bf16[1024,512]{1,0:T(8,128)(2,1)}, u32[]{:S(2)}) copy-start(bf16[1024,512]{1,0:T(8,128)(2,1)} %param.9) | copy-start | bytes 3145732
  9.5 20.6 %all-to-all-start = ((s32[64,1,2]{2,1,0:T(1,128)}), s32[64,1,2]{2,1,0:T(1,128)S(1)}, u32[]{:S(2)}, u32[]{:S(2)}) async-start(s32[64,1,2]{2,1,0:T(1,128)} %bitcast.8), calls=%async_computation | async-start | bytes 65536 | tf_op jit(solution)/shard_map/all_to_all | solution.py:123
  23.9 5.9 %copy-start.1 = (bf16[8,128,128]{2,1,0:T(8,128)(2,1)}, bf16[8,128,128]{2,1,0:T(8,128)(2,1)S(1)}, u32[]{:S(2)}) copy-start(bf16[8,128,128]{2,1,0:T(8,128)(2,1)S(1)} %multiply_convert_fusion.1.q_ref) | copy-start | bytes 786436
  30.1 10.3 %copy-start.2 = (bf16[512,128]{1,0:T(8,128)(2,1)S(1)}, bf16[512,128]{1,0:T(8,128)(2,1)}, u32[]{:S(2)}) copy-start(bf16[512,128]{1,0:T(8,128)(2,1)} %param.11) | copy-start | bytes 393220
  30.1 105.2 %all-to-all-start.1 = ((bf16[64,256,128]{2,1,0:T(8,128)(2,1)}), bf16[64,256,128]{2,1,0:T(8,128)(2,1)}, u32[]{:S(2)}, u32[]{:S(2)}) async-start(bf16[64,256,128]{2,1,0:T(8,128)(2,1)} %bitcast.48), calls=%async_computation.1 | async-start | bytes 8388608 | tf_op jit(solution)/shard_map/all_to_all | solution.py:126
  40.5 1.0 copy-start.4
  155.3 42.0 %copy-start.3 = (bf16[128,512]{1,0:T(8,128)(2,1)S(1)}, bf16[128,512]{1,0:T(8,128)(2,1)}, u32[]{:S(2)}) copy-start(bf16[128,512]{1,0:T(8,128)(2,1)} %param.13) | copy-start | bytes 393220
  155.3 142.4 %all-to-all-start.2 = ((bf16[64,272,128]{2,1,0:T(8,128)(2,1)}), bf16[64,272,128]{2,1,0:T(8,128)(2,1)}, u32[]{:S(2)}, u32[]{:S(2)}) async-start(bf16[64,272,128]{2,1,0:T(8,128)(2,1)} %shard_map.92), calls=%async_computation.2 | async-start | bytes 8912896 | tf_op jit(solution)/shard_map/all_to_all | solution.py:156
  197.2 138.7 %all-gather.2.cloned.1.call-start = ((), (), s32[]{:S(2)}) async-start(), calls=%async_computation.3 | async-start | bytes 1966080 | tf_op jit(solution)/shard_map/all_gather | solution.py:168
Sparse Core Ops, SparseCore 0:
  305.3 30.5 all-gather.1

commit v2 on v1

v2 whole, which is shorter than its diff:
```python
import functools

import jax
import jax.numpy as jnp
from jax import lax
from jax.experimental import pallas as pl
from jax.experimental.pallas import tpu as pltpu
from jax.sharding import PartitionSpec as P


def unit_rows(values, count):
    shaped = values.reshape(values.shape[0], count, -1)
    total = jnp.sum(shaped * shaped, axis=-1, keepdims=True)
    return (shaped * lax.rsqrt(total + 1e-06)).astype(jnp.bfloat16).reshape(values.shape)


def tile_kernel(pick_ref, live_ref, scale_ref, q_ref, km_ref, vt_ref, out_ref, den_scr, *, count, capacity):
    g = pl.program_id(0)
    group, feat, width = q_ref.shape
    lane_rows = lax.broadcasted_iota(jnp.int32, (count * width, 1), 0)
    scale_col = jnp.zeros((count * width, 1), jnp.float32)
    for h in range(count):
        inside = (lane_rows >= h * width) & (lane_rows < (h + 1) * width)
        scale_col = jnp.where(inside, scale_ref[h], scale_col)
    for i in range(group):
        t = g * group + i
        dest, slot = i // capacity, i % capacity

        @pl.when(live_ref[t] > 0)
        def _():
            s = jnp.dot(km_ref[pick_ref[t]], q_ref[i], preferred_element_type=jnp.float32)
            w = jnp.exp(scale_col * (s - 1.0))
            for h in range(count):
                den_scr[i * count + h:i * count + h + 1, :] = jnp.sum(
                    w[h * width:(h + 1) * width], axis=0, keepdims=True
                )
            num = jnp.dot(
                vt_ref[pick_ref[t]], w.astype(jnp.bfloat16), preferred_element_type=jnp.float32
            )
            out_ref[dest, slot * feat:(slot + 1) * feat, :] = num.astype(out_ref.dtype)

        @pl.when(live_ref[t] == 0)
        def _():
            out_ref[dest, slot * feat:(slot + 1) * feat, :] = jnp.zeros((feat, width), out_ref.dtype)
            den_scr[i * count:(i + 1) * count, :] = jnp.zeros((count, width), den_scr.dtype)

    per = capacity * count
    extra = out_ref.shape[1] - capacity * feat
    for d in range(group // capacity):
        rows = den_scr[d * per:(d + 1) * per, :]
        block = jnp.concatenate([rows, jnp.zeros((extra - per, width), rows.dtype)], axis=0)
        out_ref[d, capacity * feat:, :] = block.astype(out_ref.dtype)


def run_tiles(query_t, key_stack, value_t, pick, live, scales, capacity):
    tiles, feat, width = query_t.shape
    count = scales.shape[0]
    group = 8
    nblocks = key_stack.shape[0]
    extra = 16
    rows_out = capacity * feat + extra
    grid_spec = pltpu.PrefetchScalarGridSpec(
        num_scalar_prefetch=2,
        grid=(tiles // group,),
        in_specs=[
            pl.BlockSpec(memory_space=pltpu.SMEM),
            pl.BlockSpec((group, feat, width), lambda g, pick, live: (g, 0, 0)),
            pl.BlockSpec((nblocks, count * width, feat), lambda g, pick, live: (0, 0, 0)),
            pl.BlockSpec((nblocks, feat, count * width), lambda g, pick, live: (0, 0, 0)),
        ],
        out_specs=pl.BlockSpec((group // capacity, rows_out, width), lambda g, pick, live: (g, 0, 0)),
        scratch_shapes=[pltpu.VMEM((group * count, width), jnp.float32)],
    )
    return pl.pallas_call(
        functools.partial(tile_kernel, count=count, capacity=capacity),
        grid_spec=grid_spec,
        out_shape=jax.ShapeDtypeStruct((tiles // capacity, rows_out, width), jnp.bfloat16),
    )(pick, live, scales, query_t, key_stack, value_t)


def split_result(result, capacity, width, count):
    dests, rows_out, lanes = result.shape
    feat = (rows_out - 16) // capacity
    numer = result[:, :capacity * feat, :].reshape(dests * capacity, feat, lanes)
    denom = result[:, capacity * feat:capacity * feat + capacity * count, :]
    return numer, denom.reshape(dests * capacity, count * width)


def body(feats, w_query, w_key, w_value, w_out, head_scale, nbr_owner, nbr_local, slot_valid):
    rows = feats.shape[0]
    feat = w_query.shape[1]
    count = head_scale.shape[0]
    nblocks, slots = nbr_owner.shape
    width = rows // nblocks
    devices = lax.axis_size("nodes")
    capacity = max(2, min(nblocks // 2, 3 * nblocks * slots // (2 * devices)))
    tile_count = devices * capacity
    query_n = unit_rows(jnp.dot(feats, w_query, preferred_element_type=jnp.float32), count)
    key_n = unit_rows(jnp.dot(feats, w_key, preferred_element_type=jnp.float32), count)
    value_b = jnp.dot(feats, w_value, preferred_element_type=jnp.float32).astype(jnp.bfloat16)
    hd = feat // count
    query_t = jnp.swapaxes(query_n.reshape(nblocks, width, feat), 1, 2)
    key_blocks = key_n.reshape(nblocks, width, feat)
    value_t = jnp.swapaxes(value_b.reshape(nblocks, width, feat), 1, 2)
    head_of = jnp.arange(feat, dtype=jnp.int32) // hd
    key_stack = jnp.stack(
        [jnp.where(head_of[None, None, :] == h, key_blocks, 0) for h in range(count)], axis=1
    ).reshape(nblocks, count * width, feat)
    value_stack = jnp.stack(
        [jnp.where(head_of[None, :, None] == h, value_t, 0) for h in range(count)], axis=2
    ).reshape(nblocks, feat, count * width)
    owners = nbr_owner.reshape(-1)
    pairs = owners.shape[0]
    pair_block = jnp.arange(pairs, dtype=jnp.int32) // slots
    owner_hot = (owners[:, None] == jnp.arange(devices, dtype=jnp.int32)[None, :]).astype(jnp.int32)
    rank = jnp.sum(jnp.cumsum(owner_hot, axis=0) * owner_hot, axis=1) - 1
    target = owners * capacity + rank
    place = (target[:, None] == jnp.arange(tile_count, dtype=jnp.int32)[None, :]).astype(jnp.int32)
    wanted = jnp.where(slot_valid.reshape(-1) > 0, nbr_local.reshape(-1), -1)
    request = jnp.sum(place * (wanted[:, None] + 1), axis=0) - 1
    block_hot = (pair_block[:, None] == jnp.arange(nblocks, dtype=jnp.int32)[None, :]).astype(
        jnp.float32
    )
    selector_onehot = jnp.dot(place.T.astype(jnp.float32), block_hot).astype(jnp.bfloat16)
    query_outgoing = jnp.einsum(
        "cm,mfq->cfq", selector_onehot, query_t, preferred_element_type=jnp.float32
    ).astype(jnp.bfloat16)
    asked = lax.all_to_all(
        request.reshape(devices, capacity), "nodes", split_axis=0, concat_axis=0, tiled=True
    ).reshape(-1)
    query_in = lax.all_to_all(
        query_outgoing.reshape(devices, capacity * feat, width),
        "nodes",
        split_axis=0,
        concat_axis=0,
        tiled=True,
    )
    self_numer, self_denom = split_result(
        run_tiles(
            query_t,
            key_stack,
            value_stack,
            jnp.arange(nblocks, dtype=jnp.int32),
            jnp.ones((nblocks,), jnp.int32),
            head_scale,
            capacity,
        ),
        capacity,
        width,
        count,
    )
    live_in = (asked >= 0).astype(jnp.int32)
    pick_in = jnp.clip(asked, 0, nblocks - 1)
    result = run_tiles(
        query_in.reshape(tile_count, feat, width),
        key_stack,
        value_stack,
        pick_in,
        live_in,
        head_scale,
        capacity,
    )
    result = lax.all_to_all(result, "nodes", split_axis=0, concat_axis=0, tiled=True)
    numer, denom = split_result(result, capacity, width, count)
    numer_total = self_numer.astype(jnp.float32) + jnp.einsum(
        "ub,ufq->bfq", selector_onehot, numer, preferred_element_type=jnp.float32
    )
    numer_total = jnp.swapaxes(numer_total, 1, 2)
    denominator_overall = self_denom.astype(jnp.float32) + jnp.einsum(
        "uq,ul->ql", selector_onehot, denom, preferred_element_type=jnp.float32
    )
    den_rows = jnp.transpose(denominator_overall.reshape(nblocks, count, width), (0, 2, 1))
    attn = numer_total.reshape(nblocks, width, count, feat // count) / den_rows[..., None]
    attn = attn.astype(jnp.bfloat16).reshape(rows, feat)
    attn_all = lax.all_gather(attn, "heads", axis=1, tiled=True)
    w_cols = lax.dynamic_slice_in_dim(w_out, lax.axis_index("heads") * feat, feat, axis=1)
    return jnp.dot(attn_all, w_cols, preferred_element_type=jnp.float32).astype(jnp.bfloat16)


def solution(mesh):
    placed = (
        P("nodes", None),
        P(None, "heads"),
        P(None, "heads"),
        P(None, "heads"),
        P(None, None),
        P("heads"),
        P("nodes", None),
        P("nodes", None),
        P("nodes", None),
    )
    return jax.shard_map(
        body, mesh=mesh, in_specs=placed, out_specs=P("nodes", "heads"), check_vma=False
    )
```

time: 347 us -> 322 us (0.928)
  waiting for transfers between devices: 213 us -> 192 us
  blocking collectives: 0 us -> 14.1 us
  starting transfers between devices: 64.3 us -> 52.3 us
  Pallas kernels: 27 us -> 20.9 us
    all_gather x1, waiting for transfers between devices: 30.7 us -> 10.5 us  [body(): attn_all = lax.all_gather(attn, 'heads', axis=1, tiled=True)]
    unnamed x0 -> x1, blocking collectives: none -> 14.1 us
    all_to_all x1, starting transfers between devices: 41.9 us -> 29.8 us  [body(): lax.all_to_all(result, 'nodes', split_axis=0, concat_axis=0, tiled=True)]
    pallas_call x2, Pallas kernels: 27 us -> 20.9 us  [run_tiles(): pl.pallas_call(functools.partial(tile_kernel, count=count, capacity=capac...]
  transfers between devices with their start and end apart: 4 -> 4, of which waited for: 4 -> 4; matrix products, arithmetic and copies ran while one was open for 4% -> 5% of each run, Pallas kernels for 2% -> 2%
where the time goes in v2:
time: 322 us
  waiting for transfers between devices  192 us (60%)
  starting transfers between devices  52.3 us (16%)
  Pallas kernels  20.9 us (6%)
  local copies, waits for them, and re-layouts  15.9 us (5%)
  blocking collectives  14.1 us (4%)
  between operations  13.7 us (4%)
  matrix products  8.79 us (3%)
  other arithmetic  4.64 us (1%)
    all_to_all x1, waiting for transfers between devices, body(): lax.all_to_all(result, 'nodes', split_axis=0, concat_axis=0, tiled=True)  92.3 us
    all_to_all x1, waiting for transfers between devices, body(): lax.all_to_all(query_outgoing.reshape(devices, capacity * feat, width), '...  88.9 us
    all_to_all x1, starting transfers between devices, body(): lax.all_to_all(result, 'nodes', split_axis=0, concat_axis=0, tiled=True)  29.8 us
    pallas_call x2, Pallas kernels, run_tiles(): pl.pallas_call(functools.partial(tile_kernel, count=count, capacity=capac...  20.9 us
    unnamed x1, blocking collectives  14.1 us
    all_to_all x1, starting transfers between devices, body(): lax.all_to_all(request.reshape(devices, capacity), 'nodes', split_axis=0,...  12 us
    all_gather x1, waiting for transfers between devices, body(): attn_all = lax.all_gather(attn, 'heads', axis=1, tiled=True)  10.5 us
    all_to_all x1, starting transfers between devices, body(): lax.all_to_all(query_outgoing.reshape(devices, capacity * feat, width), '...  10.4 us
  transfers between devices with their start and end apart: 4, of which 4 were waited for; matrix products, arithmetic and copies ran while one was open for 5% of the time, Pallas kernels for 2%

profile of v2, /device:TPU:2, one launch (start us, length us, event | category | flops | bytes accessed | tf_op | source)
XLA Modules:
  0.0 322.2 jit_solution(12237097005673881210)
XLA Ops:
  6.5 0.0 copy-start
  6.5 0.8 copy.59
  7.4 0.1 reshape.209
  7.5 0.1 fusion.16
  7.5 0.1 reduce_window_sum.11
  7.6 0.2 select_reduce_fusion.1
  7.8 0.7 select_add_fusion
  8.5 0.1 copy.60
  8.6 0.1 add.83
  8.7 0.1 select_reduce_fusion
  8.8 0.8 sub.32
  9.5 12.0 %all-to-all-start = ((s32[64,1,2]{2,1,0:T(1,128)}), s32[64,1,2]{2,1,0:T(1,128)S(1)}, u32[]{:S(2)}, u32[]{:S(2)}) async-start(s32[64,1,2]{2,1,0:T(1,128)} %bitcast.13), calls=%async_computation | async-start | bytes 65536 | tf_op jit(solution)/shard_map/all_to_all | solution.py:128
  21.6 0.0 copy-done
  21.6 1.3 fusion.22
  22.9 0.2 copy.51
  23.1 0.2 copy.50
  23.4 0.1 copy.67
  23.6 0.2 convolution_convert_fusion.3
  23.8 0.1 fusion.9.q_ref
  23.9 0.0 copy-start.1
  23.9 1.3 convolution_convert_fusion
  25.2 4.6 %copy.63 = bf16[128,128,128]{2,1,0:T(8,128)(2,1)} copy(bf16[128,128,128]{2,0,1:T(8,128)(2,1)S(1)} %convolution_convert_fusion) | data formatting | bytes 8388608 | tf_op jit(solution)/shard_map/convert_element_type | solution.py:127
  29.9 0.0 copy-done.1
  29.9 0.3 all-to-all-done
  30.2 10.4 %all-to-all-start.1 = ((bf16[64,256,128]{2,1,0:T(8,128)(2,1)}), bf16[64,256,128]{2,1,0:T(8,128)(2,1)}, u32[]{:S(2)}, u32[]{:S(2)}) async-start(bf16[64,256,128]{2,1,0:T(8,128)(2,1)} %bitcast.76), calls=%async_computation.1 | async-start | bytes 8388608 | tf_op jit(solution)/shard_map/all_to_all | solution.py:131
  40.6 0.0 copy-done.2
  40.6 0.4 fusion.23
  41.0 0.0 copy-start.4
  41.0 0.2 copy.54
  41.2 0.2 copy.53
  41.6 0.1 copy.68
  41.7 0.2 broadcast_select_fusion.1
  41.9 0.2 broadcast_select_fusion
  42.1 0.1 pad_maximum_fusion
  42.2 1.2 copy.55
  43.4 0.0 copy-done.4
  43.4 0.4 convolution_convert_fusion.2
  43.8 0.2 copy.56
  44.0 0.1 select_bitcast_fusion.1
  44.1 0.9 copy_bitcast_fusion.vt_ref
  45.0 0.2 fusion.14
  45.2 0.6 min.12.pick_ref
  45.8 0.7 reshape.217.live_ref
  46.5 88.9 %all-to-all-done.1 = bf16[64,256,128]{2,1,0:T(8,128)(2,1)} async-done(((bf16[64,256,128]{2,1,0:T(8,128)(2,1)}), bf16[64,256,128]{2,1,0:T(8,128)(2,1)}, u32[]{:S(2)}, u32[]{:S(2)}) %all-to-all-start.1) | async-done | bytes 4194336 | tf_op jit(solution)/shard_map/all_to_all | solution.py:131
  135.4 15.6 %shard_map.92 = bf16[64,272,128]{2,1,0:T(8,128)(2,1)} custom-call(s32[128]{0:T(128)} %min.12.pick_ref, s32[128]{0:T(128)} %reshape.217.live_ref, f32[2]{0:T(128)} %scale_ref.3, bf16[128,128,128]{2,1,0:T(8,128)(2,1)} %bitcast.15.q_ref, bf16[8,256,128]{2,1,0:T(8,128)(2,1)} %bitcast.78, bf16[8,128,256]{2,1,0:T(8,128)(2,1)} %copy_bitcast_fusion.vt_ref), custom_call_target="tpu_custom_call" | custom-call | tf_op jit(solution)/shard_map/pallas_call | solution.py:74
  151.0 29.8 %all-to-all-start.2 = ((bf16[64,272,128]{2,1,0:T(8,128)(2,1)}), bf16[64,272,128]{2,1,0:T(8,128)(2,1)}, u32[]{:S(2)}, u32[]{:S(2)}) async-start(bf16[64,272,128]{2,1,0:T(8,128)(2,1)} %shard_map.92), calls=%async_computation.2 | async-start | bytes 8912896 | tf_op jit(solution)/shard_map/all_to_all | solution.py:163
  180.8 0.0 all-gather.3.cloned.1.call-start
  180.8 0.5 iota.38.pick_ref
  181.4 0.6 broadcast_2_live_ref.2.live_ref
  182.0 5.3 %shard_map.91 = bf16[4,272,128]{2,1,0:T(8,128)(2,1)} custom-call(s32[8]{0:T(128)} %iota.38.pick_ref, s32[8]{0:T(128)} %broadcast_2_live_ref.2.live_ref, f32[2]{0:T(128)} %scale_ref.3, bf16[8,128,128]{2,1,0:T(8,128)(2,1)} %copy-done.1, bf16[8,256,128]{2,1,0:T(8,128)(2,1)} %bitcast.79, bf16[8,128,256]{2,1,0:T(8,128)(2,1)} %copy_bitcast_fusion.vt_ref), custom_call_target="tpu_custom_call" | custom-call | tf_op jit(solution)/shard_map/pallas_call | solution.py:74
  187.3 1.0 slice.16
  188.2 0.7 slice_convert_fusion
  189.0 92.3 %all-to-all-done.2 = bf16[64,272,128]{2,1,0:T(8,128)(2,1)} async-done(((bf16[64,272,128]{2,1,0:T(8,128)(2,1)}), bf16[64,272,128]{2,1,0:T(8,128)(2,1)}, u32[]{:S(2)}, u32[]{:S(2)}) %all-to-all-start.2) | async-done | bytes 4456480 | tf_op jit(solution)/shard_map/all_to_all | solution.py:163
  281.3 0.9 slice.19
  282.3 0.1 fusion.5
  282.4 2.5 slice.17
  284.9 0.0 copy-start.3
  284.9 2.5 fusion.2
  287.5 0.9 fusion.6
  288.3 0.0 all-gather.3.cloned.1.call-update
  288.4 0.0 copy-done.3
  288.4 14.1 %all-gather = bf16[512,512]{1,0:T(8,128)(2,1)S(1)} all-gather(bf16[128,512]{1,0:T(8,128)(2,1)S(1)} %copy-done.3), channel_id=2, replica_groups=mesh['nodes'=64,'heads'=4] {'heads'}, dimensions={0}, use_global_device_ids=true | all-gather | bytes 655360 | tf_op args[4]
  302.4 10.5 %all-gather.3.cloned.1.call-done = bf16[1024,512]{0,1:T(8,128)(2,1)} async-done(((bf16[1024,128]{0,1:T(8,128)(2,1)}), bf16[1024,512]{0,1:T(8,128)(2,1)}) %all-gather.3.cloned.1.call-update) | async-done | bytes 1048592 | tf_op jit(solution)/shard_map/all_gather | solution.py:175
  312.9 2.4 convolution_convert_fusion.1
  (14 shorter events, 0.4 us)
Async XLA Ops:
  6.5 15.0 %copy-start = (bf16[1024,512]{1,0:T(8,128)(2,1)S(1)}, bf16[1024,512]{1,0:T(8,128)(2,1)}, u32[]{:S(2)}) copy-start(bf16[1024,512]{1,0:T(8,128)(2,1)} %param.9) | copy-start | bytes 3145732
  9.5 20.6 %all-to-all-start = ((s32[64,1,2]{2,1,0:T(1,128)}), s32[64,1,2]{2,1,0:T(1,128)S(1)}, u32[]{:S(2)}, u32[]{:S(2)}) async-start(s32[64,1,2]{2,1,0:T(1,128)} %bitcast.13), calls=%async_computation | async-start | bytes 65536 | tf_op jit(solution)/shard_map/all_to_all | solution.py:128
  23.9 5.9 %copy-start.1 = (bf16[8,128,128]{2,1,0:T(8,128)(2,1)}, bf16[8,128,128]{2,1,0:T(8,128)(2,1)S(1)}, u32[]{:S(2)}) copy-start(bf16[8,128,128]{2,1,0:T(8,128)(2,1)S(1)} %fusion.9.q_ref) | copy-start | bytes 786436
  30.2 10.4 %copy-start.2 = (bf16[512,128]{1,0:T(8,128)(2,1)S(1)}, bf16[512,128]{1,0:T(8,128)(2,1)}, u32[]{:S(2)}) copy-start(bf16[512,128]{1,0:T(8,128)(2,1)} %param.11) | copy-start | bytes 393220
  30.2 105.3 %all-to-all-start.1 = ((bf16[64,256,128]{2,1,0:T(8,128)(2,1)}), bf16[64,256,128]{2,1,0:T(8,128)(2,1)}, u32[]{:S(2)}, u32[]{:S(2)}) async-start(bf16[64,256,128]{2,1,0:T(8,128)(2,1)} %bitcast.76), calls=%async_computation.1 | async-start | bytes 8388608 | tf_op jit(solution)/shard_map/all_to_all | solution.py:131
  41.0 2.4 copy-start.4
  151.0 130.3 %all-to-all-start.2 = ((bf16[64,272,128]{2,1,0:T(8,128)(2,1)}), bf16[64,272,128]{2,1,0:T(8,128)(2,1)}, u32[]{:S(2)}, u32[]{:S(2)}) async-start(bf16[64,272,128]{2,1,0:T(8,128)(2,1)} %shard_map.92), calls=%async_computation.2 | async-start | bytes 8912896 | tf_op jit(solution)/shard_map/all_to_all | solution.py:163
  180.8 132.1 %all-gather.3.cloned.1.call-start = ((), (), s32[]{:S(2)}) async-start(), calls=%async_computation.3 | async-start | bytes 1310720 | tf_op jit(solution)/shard_map/all_gather | solution.py:175
  284.9 3.5 %copy-start.3 = (bf16[128,512]{1,0:T(8,128)(2,1)S(1)}, bf16[128,512]{1,0:T(8,128)(2,1)}, u32[]{:S(2)}) copy-start(bf16[128,512]{1,0:T(8,128)(2,1)} %param.13) | copy-start | bytes 393220
Sparse Core Ops, SparseCore 0:
  288.5 24.4 all-gather.2
